TPU v7x, 256 devices: a whole 4x4x8 slice. The times are simulated.
256 devices in a mesh: seq: 64 (over x, z, core), head: 4 (over y).
Axes of the slice: x: 4, y: 4, z: 8, core: 2. Of those that a mesh axis runs over, the one named last changes fastest.
Arguments:
- acceptance_linear: bfloat16 [32768, 4096], P(('seq', 'head')), may hold values from -6 to 6
- lookup_linear: bfloat16 [32768, 4096], P(('seq', 'head')), may hold values from -6 to 6
- payload_linear: bfloat16 [32768, 4096], P(('seq', 'head')), may hold values from -6 to 6
- valve_linear: bfloat16 [32768, 4096], P(('seq', 'head')), may hold values from -6 to 6
- layer_entries: bfloat16 [32768, 4096], P(('seq', 'head')), may hold values from -6 to 6
- prompt_label: int32 [32768], replicated, may hold values from 0 to 15, never falling along the last dimension, each value on 1 to 8192 neighbouring positions
- fading_baseline: float32 [4096], replicated, may hold values from -12 to -3
- previous_mixing_share: float32 [4096], replicated, may hold values from 0.2 to 0.9
- fading_lower_map: bfloat16 [4096, 128], replicated, may hold values from -0.09375 to 0.09375
- fading_raise_map: bfloat16 [128, 4096], replicated, may hold values from -0.5 to 0.5
- diagonal_reward: float32 [4096], replicated, may hold values from -0.5 to 1
- cluster_gain_vector: float32 [4096], replicated, may hold values from 0.25 to 1.75
- cluster_mean_shift_add: float32 [4096], replicated, may hold values from -1.5 to 1.5
Outputs:
- gated: bfloat16 [32768, 4096], P(('seq', 'head'))
All inputs are finite; a program needn't handle non-finite values.
Results may differ from a plain program's by a relative error of at most 0.001.
The roundings to bfloat16 on the way count: a program that leaves them out, or rounds other values in their place, can miss the bound.
Values may be sent and summed in bfloat16 or wider, within the bound.
No kernel may reach another device: no remote copies, remote signals or barrier semaphores. Data moves between devices by JAX's collectives and lax.ppermute only.
A program may use at most 192 MiB of HBM per device.

v0:
```python
import jax
import jax.numpy as jnp
from jax import lax
from jax.sharding import PartitionSpec as P

ATTENTION_SPAN = 64
CH = 128
norm_eps = 0.00064
decay_floor = -0.5
highest = lax.Precision.HIGHEST


def shifted(value, axis, by):
    size = lax.axis_size(axis)
    pairs = [(i, i + by) for i in range(size) if 0 <= i + by < size]
    return lax.ppermute(value, axis, pairs)


def earlier_segment(prompt_label, position):
    earlier = lax.dynamic_slice_in_dim(prompt_label, jnp.maximum(position - 1, 0), 1, 0)
    return jnp.where(position > 0, earlier, jnp.full_like(earlier, -1))


def local(
    acceptance_linear,
    lookup_linear,
    payload_linear,
    valve_linear,
    layer_entries,
    prompt_label,
    fading_baseline,
    previous_mixing_share,
    fading_lower_map,
    fading_raise_map,
    diagonal_reward,
    cluster_gain_vector,
    cluster_mean_shift_add,
):
    head_count = lax.axis_size("head")
    seq_index = lax.axis_index("seq")
    head_index = lax.axis_index("head")
    row_count = layer_entries.shape[0]
    block_start = (seq_index * head_count + head_index) * row_count
    own_seg = lax.dynamic_slice_in_dim(prompt_label, block_start, row_count, 0)
    prior_seg = jnp.concatenate([earlier_segment(prompt_label, block_start), own_seg[:-1]])
    edge_row = shifted(layer_entries[-1:], ("seq", "head"), 1)
    prev_rows = jnp.concatenate([edge_row, layer_entries[:-1]], axis=0)
    prev_rows = jnp.where((prior_seg == own_seg)[:, None], prev_rows, jnp.zeros_like(prev_rows))
    current = layer_entries.astype(jnp.float32)
    blended_input = (
        current + (prev_rows.astype(jnp.float32) - current) * previous_mixing_share
    ).astype(jnp.bfloat16)
    decay_hidden_rows = jnp.tanh(
        jnp.dot(blended_input, fading_lower_map, preferred_element_type=jnp.float32)
    ).astype(jnp.bfloat16)
    decay_score = fading_baseline + jnp.dot(
        decay_hidden_rows, fading_raise_map, preferred_element_type=jnp.float32
    )
    log_decay = jnp.maximum(-jnp.exp(decay_score), decay_floor).astype(jnp.bfloat16)
    query_head, key_head, value_head, decay_head = (
        lax.all_to_all(acceptance_linear, "head", split_axis=1, concat_axis=0, tiled=True),
        lax.all_to_all(lookup_linear, "head", split_axis=1, concat_axis=0, tiled=True),
        lax.all_to_all(payload_linear, "head", split_axis=1, concat_axis=0, tiled=True),
        lax.all_to_all(log_decay, "head", split_axis=1, concat_axis=0, tiled=True),
    )
    tokens = query_head.shape[0]
    partition_extent = query_head.shape[1]
    local_heads = partition_extent // ATTENTION_SPAN
    stretches = tokens // CH
    seq_start = seq_index * tokens
    seg_block = lax.dynamic_slice_in_dim(prompt_label, seq_start, tokens, 0).reshape(stretches, CH)
    seg_before = earlier_segment(prompt_label, seq_start)
    stretch_prior = jnp.concatenate([seg_before, seg_block[:-1, -1]])
    feature_start = head_index * partition_extent
    partition_reward = lax.dynamic_slice_in_dim(
        diagonal_reward, feature_start, partition_extent, 0
    ).reshape(local_heads, ATTENTION_SPAN)
    gain_local = lax.dynamic_slice_in_dim(
        cluster_gain_vector, feature_start, partition_extent, 0
    ).reshape(local_heads, ATTENTION_SPAN)
    bias_local = lax.dynamic_slice_in_dim(
        cluster_mean_shift_add, feature_start, partition_extent, 0
    ).reshape(local_heads, ATTENTION_SPAN)
    blocked = (stretches, CH, local_heads, ATTENTION_SPAN)
    request_vectors = query_head.reshape(blocked).astype(jnp.float32)
    lookup_vectors = key_head.reshape(blocked).astype(jnp.float32)
    payload_vectors = value_head.reshape(blocked).astype(jnp.float32)
    decays = decay_head.reshape(blocked).astype(jnp.float32)
    cumulative = jnp.cumsum(decays, axis=1)
    before = cumulative - decays
    ending = cumulative[:, -1]
    scaled_query = request_vectors * jnp.exp(before)
    scaled_key = lookup_vectors * jnp.exp(-cumulative)
    scores = jnp.einsum("cthd,cshd->chts", scaled_query, scaled_key, precision=highest)
    causal = lax.broadcasted_iota(jnp.int32, (CH, CH), 0) > lax.broadcasted_iota(
        jnp.int32, (CH, CH), 1
    )
    allowed = causal[None] & (seg_block[:, :, None] == seg_block[:, None, :])
    scores = jnp.where(allowed[:, None], scores, jnp.zeros_like(scores))
    within = jnp.einsum("chts,cshd->cthd", scores, payload_vectors, precision=highest)
    diagonal_contribution = (
        jnp.sum(request_vectors * partition_reward * lookup_vectors, axis=3, keepdims=True)
        * payload_vectors
    )
    keep_last = (seg_block == seg_block[:, -1:]).astype(jnp.float32)
    tail_keys = lookup_vectors * jnp.exp(ending[:, None] - cumulative) * keep_last[:, :, None, None]
    stretch_state = jnp.einsum("cthd,cthe->chde", tail_keys, payload_vectors, precision=highest)
    stretch_decay = (
        jnp.exp(ending) * (seg_block[:, -1] == stretch_prior).astype(jnp.float32)[:, None, None]
    )

    def advance(carry_state, pieces):
        factor, new_part = pieces
        return (factor[:, :, None] * carry_state + new_part, carry_state)

    zero_state = jnp.zeros((local_heads, ATTENTION_SPAN, ATTENTION_SPAN), jnp.float32)
    span_state, local_start = lax.scan(advance, zero_state, (stretch_decay, stretch_state))

    def multiply(product, factor):
        return (product * factor, product)

    span_decay, decay_before = lax.scan(
        multiply, jnp.ones((local_heads, ATTENTION_SPAN), jnp.float32), stretch_decay
    )
    seq_count = lax.axis_size("seq")
    packed = jnp.concatenate([span_state, span_decay[:, None, :]], axis=1)

    def unpack(value):
        return (value[:, :ATTENTION_SPAN], value[:, ATTENTION_SPAN])

    prior_state, prior_decay = unpack(shifted(packed, "seq", 1))
    incoming, cover = (prior_state, prior_decay)
    reach = 1
    if seq_count > 2:
        far_state, far_decay = unpack(shifted(packed, "seq", 2))
        incoming = prior_decay[:, :, None] * far_state + prior_state
        cover = prior_decay * far_decay
        reach = 2
    while reach < seq_count - 1:
        far_state, far_decay = unpack(
            shifted(jnp.concatenate([incoming, cover[:, None, :]], axis=1), "seq", reach)
        )
        incoming = cover[:, :, None] * far_state + incoming
        cover = cover * far_decay
        reach *= 2
    start_state = local_start + decay_before[:, :, :, None] * incoming[None]
    keep_first = (seg_block == stretch_prior[:, None]).astype(jnp.float32)
    carried = jnp.einsum(
        "cthd,chde->cthe",
        scaled_query * keep_first[:, :, None, None],
        start_state,
        precision=highest,
    )
    mixing = within + diagonal_contribution + carried
    center = mixing - jnp.mean(mixing, axis=3, keepdims=True)
    spread = jnp.mean(center * center, axis=3, keepdims=True)
    normed = center * lax.rsqrt(spread + norm_eps) * gain_local + bias_local
    normed = normed.astype(jnp.bfloat16).reshape(tokens, partition_extent)
    returned = lax.all_to_all(normed, "head", split_axis=0, concat_axis=1, tiled=True)
    return (returned.astype(jnp.float32) * jax.nn.silu(valve_linear.astype(jnp.float32))).astype(
        jnp.bfloat16
    )


def solution(mesh):
    return jax.shard_map(
        local,
        mesh=mesh,
        in_specs=(
            P(("seq", "head"), None),
            P(("seq", "head"), None),
            P(("seq", "head"), None),
            P(("seq", "head"), None),
            P(("seq", "head"), None),
            P(),
            P(),
            P(),
            P(),
            P(),
            P(),
            P(),
            P(),
        ),
        out_specs=P(("seq", "head"), None),
        check_vma=False,
    )
```

profile of v0, /device:TPU:162, one launch (start us, length us, event | category | flops | bytes accessed | tf_op | source)
XLA Modules:
  0.0 318.2 jit_solution(3429438494521364704)
XLA Ops:
  0.0 2.4 copy.126
  2.4 4.5 %all-to-all-start = ((bf16[128,4,1024]{0,2,1:T(8,128)(2,1)}), bf16[128,4,1024]{0,2,1:T(8,128)(2,1)S(1)}, u32[]{:S(2)}, u32[]{:S(2)}) async-start(bf16[128,4,1024]{0,2,1:T(8,128)(2,1)} %bitcast.1), calls=%async_computation | async-start | bytes 2097152 | tf_op jit(solution)/shard_map/all_to_all | solution.py:61
  6.9 1.3 copy.131
  8.2 13.8 %all-to-all-done = bf16[128,4,1024]{0,2,1:T(8,128)(2,1)S(1)} async-done(((bf16[128,4,1024]{0,2,1:T(8,128)(2,1)}), bf16[128,4,1024]{0,2,1:T(8,128)(2,1)S(1)}, u32[]{:S(2)}, u32[]{:S(2)}) %all-to-all-start) | async-done | bytes 1048608 | tf_op jit(solution)/shard_map/all_to_all | solution.py:61
  22.0 3.5 %all-to-all-start.2 = ((bf16[128,4,1024]{0,2,1:T(8,128)(2,1)}), bf16[128,4,1024]{0,2,1:T(8,128)(2,1)S(1)}, u32[]{:S(2)}, u32[]{:S(2)}) async-start(bf16[128,4,1024]{0,2,1:T(8,128)(2,1)} %bitcast.88), calls=%async_computation.2 | async-start | bytes 2097152 | tf_op jit(solution)/shard_map/all_to_all | solution.py:62
  26.4 3.9 %collective-permute-start = (bf16[1,4096]{1,0:T(2,128)(2,1)S(1)}, bf16[1,4096]{1,0:T(2,128)(2,1)S(1)}, u32[]{:S(2)}, u32[]{:S(2)}) collective-permute-start(bf16[1,4096]{1,0:T(2,128)(2,1)S(1)} %slice.59), channel_id=1, source_target_pairs={{0,1},{1,2},{2,3},{3,4},{4,5},{5,6},{6,7},{7,8},{8,9},{9,10},{10,1... | collective-permute-start | bytes 24584 | tf_op jit(solution)/shard_map/ppermute | solution.py:16
  31.1 1.4 fusion.55
  34.0 2.5 collective-permute-done
  36.4 4.3 %fusion.4 = bf16[128,4096]{1,0:T(8,128)(2,1)} fusion(bf16[128,4096]{1,0:T(8,128)(2,1)S(1)} %copy-done, bf16[4096,128]{1,0:T(8,128)(2,1)} %param.25, bf16[128,4096]{1,0:T(8,128)(2,1)} %param.21, bf16[127,4096]{1,0:T(8,128)(2,1)} %bitcast.92, bf16[1,4096]{1,0:T(2,128)(2,1)S(1)} %collective-permute-done, f32[4096]{0:T(1024)S(1)} %copy-done.15, ...), kind=kOutput, calls=%fused_computation.10 | convolution fusion | flops 276316160 | bytes 5275776 | tf_op jit(solution)/shard_map/dot_general | solution.py:56
  40.7 2.4 copy.156
  43.1 5.5 %all-to-all-start.1 = ((bf16[128,4,1024]{0,2,1:T(8,128)(2,1)}), bf16[128,4,1024]{0,2,1:T(8,128)(2,1)}, u32[]{:S(2)}, u32[]{:S(2)}) async-start(bf16[128,4,1024]{0,2,1:T(8,128)(2,1)} %bitcast.5), calls=%async_computation.1 | async-start | bytes 2097152 | tf_op jit(solution)/shard_map/all_to_all | solution.py:64
  48.6 1.3 copy.157
  52.5 1.4 convert_element_type.112
  53.9 3.0 copy.130
  56.8 2.8 convert_element_type.114
  59.6 4.0 %copy.132 = f32[4,128,16,64]{3,2,1,0:T(8,128)} copy(f32[4,128,16,64]{1,3,2,0:T(8,128)} %bitcast.82) | data formatting | bytes 4194304 | tf_op jit(solution)/shard_map/convert_element_type | solution.py:86
  64.2 4.2 %all-to-all-start.3 = ((bf16[128,4,1024]{0,2,1:T(8,128)(2,1)}), bf16[128,4,1024]{0,2,1:T(8,128)(2,1)}, u32[]{:S(2)}, u32[]{:S(2)}) async-start(bf16[128,4,1024]{0,2,1:T(8,128)(2,1)} %bitcast.87), calls=%async_computation.3 | async-start | bytes 2097152 | tf_op jit(solution)/shard_map/all_to_all | solution.py:63
  68.4 2.7 convert_element_type.113
  71.2 4.1 %copy.128 = f32[4,128,16,64]{3,2,1,0:T(8,128)} copy(f32[4,128,16,64]{1,3,2,0:T(8,128)} %bitcast.84) | data formatting | bytes 4194304 | tf_op jit(solution)/shard_map/convert_element_type | solution.py:88
  75.3 2.5 fusion.57
  77.9 2.1 copy-done.3
  80.4 11.3 %exponential_multiply_fusion = (f32[4,128,16,64]{3,2,1,0:T(8,128)}, f32[4,128,16,64]{3,2,1,0:T(8,128)}, f32[4,128,16,64]{3,2,1,0:T(8,128)}, f32[4,128,16,64]{3,2,1,0:T(8,128)}) fusion(f32[4,128,16,64]{3,2,1,0:T(8,128)} %copy.132, f32[4,128,16,64]{3,2,1,0:T(8,128)} %copy-done.3, f32[4,128]{1,0:T(4,128)S(1)} %get-tuple-element.125, ...), kind=kLoop, calls=%fused_computation.21 | loop fusion | flops 4194304 | bytes 16797696 | tf_op jit(solution)/shard_map/mul | solution.py:93
  91.8 7.8 %fusion.7 = f32[4,16,64,64]{3,2,1,0:T(8,128)} fusion(bf16[4,128,16,64]{1,3,2,0:T(8,128)(2,1)} %bitcast.14, f32[4,128,16,64]{3,2,1,0:T(8,128)} %get-tuple-element.120), kind=kOutput, calls=%fused_computation.13 | convolution fusion | flops 402653184 | bytes 4194304 | tf_op jit(solution)/shard_map/cthd,cthe->chde/dot_general | solution.py:107
  99.6 8.8 %while.26 = (s32[]{:T(128)}, f32[16,64,64]{2,1,0:T(8,128)S(1)}, f32[4,16,64,64]{3,2,1,0:T(8,128)}, f32[4,16,64]{2,1,0:T(8,128)S(1)}, f32[4,16,64,64]{3,2,1,0:T(8,128)}, /*index=5*/s32[]{:T(128)}, s32[]{:T(128)}) while((s32[]{:T(128)}, f32[16,64,64]{2,1,0:T(8,128)S(1)}, f32[4,16,64,64]{3,2,1,0:T(8,128)}, ...), condition=%wide.region_3.4_spmd.clone, body=%wide.region_2.3_spmd.clone.sunk | while | flops 262147 | bytes 1585260 | solution.py:117
  100.5 1.3 bitcast_add_fusion.4
  102.7 1.3 bitcast_add_fusion.4
  104.9 1.3 bitcast_add_fusion.4
  107.1 1.3 bitcast_add_fusion.4
  109.5 2.1 pad_maximum_fusion
  111.5 2.9 collective-permute-start.2
  114.4 2.1 collective-permute-start.1
  116.5 11.9 %collective-permute-done.2 = f32[16,65,64]{1,2,0:T(8,128)S(1)} collective-permute-done((f32[16,65,64]{1,2,0:T(8,128)}, f32[16,65,64]{1,2,0:T(8,128)S(1)}, u32[]{:S(2)}, u32[]{:S(2)}) %collective-permute-start.2) | collective-permute-done | bytes 266272 | tf_op jit(solution)/shard_map/ppermute | solution.py:16
  129.4 1.2 copy.160
  130.6 1.9 collective-permute-done.1
  133.6 1.2 copy.159
  134.8 1.1 copy.142
  135.9 1.1 slice_add_fusion
  137.0 1.2 pad_maximum_fusion.1
  138.3 2.9 collective-permute-start.3
  141.2 11.5 %collective-permute-done.3 = f32[16,65,64]{1,2,0:T(8,128)S(1)} collective-permute-done((f32[16,65,64]{1,2,0:T(8,128)S(1)}, f32[16,65,64]{1,2,0:T(8,128)S(1)}, u32[]{:S(2)}, u32[]{:S(2)}) %collective-permute-start.3) | collective-permute-done | bytes 266272 | tf_op jit(solution)/shard_map/ppermute | solution.py:16
  153.9 1.1 copy.144
  155.0 1.1 fusion.47
  156.1 1.2 pad_maximum_fusion.2
  157.4 2.7 collective-permute-start.4
  160.1 24.8 %collective-permute-done.4 = f32[16,65,64]{1,2,0:T(8,128)S(1)} collective-permute-done((f32[16,65,64]{1,2,0:T(8,128)S(1)}, f32[16,65,64]{1,2,0:T(8,128)S(1)}, u32[]{:S(2)}, u32[]{:S(2)}) %collective-permute-start.4) | collective-permute-done | bytes 266272 | tf_op jit(solution)/shard_map/ppermute | solution.py:16
  187.1 1.1 fusion.46
  188.2 2.0 pad_maximum_fusion.3
  190.3 11.2 %collective-permute-start.5 = (f32[16,65,64]{1,2,0:T(8,128)}, f32[16,65,64]{1,2,0:T(8,128)S(1)}, u32[]{:S(2)}, u32[]{:S(2)}) collective-permute-start(f32[16,65,64]{1,2,0:T(8,128)} %pad_maximum_fusion.3), channel_id=1, source_target_pairs={{0,32},{4,36},{8,40},{12,44},{16,48},{20,52},{24,56},{28,60},{32,6... | collective-permute-start | bytes 798728 | tf_op jit(solution)/shard_map/ppermute | solution.py:16
  203.9 16.0 %collective-permute-done.5 = f32[16,65,64]{1,2,0:T(8,128)S(1)} collective-permute-done((f32[16,65,64]{1,2,0:T(8,128)}, f32[16,65,64]{1,2,0:T(8,128)S(1)}, u32[]{:S(2)}, u32[]{:S(2)}) %collective-permute-start.5) | collective-permute-done | bytes 266272 | tf_op jit(solution)/shard_map/ppermute | solution.py:16
  220.9 1.2 copy.163
  222.2 1.1 copy.148
  223.3 1.3 fusion.45
  224.5 1.2 pad_maximum_fusion.4
  225.8 7.2 %collective-permute-start.6 = (f32[16,65,64]{1,2,0:T(8,128)S(1)}, f32[16,65,64]{1,2,0:T(8,128)S(1)}, u32[]{:S(2)}, u32[]{:S(2)}) collective-permute-start(f32[16,65,64]{1,2,0:T(8,128)S(1)} %pad_maximum_fusion.4), channel_id=1, source_target_pairs={{0,64},{4,68},{8,72},{12,76},{16,80},{20,84},{24,88},{28,92},{32,9... | collective-permute-start | bytes 798728 | tf_op jit(solution)/shard_map/ppermute | solution.py:16
  233.0 1.8 fusion
  234.8 8.0 %collective-permute-done.6 = f32[16,65,64]{1,2,0:T(8,128)S(1)} collective-permute-done((f32[16,65,64]{1,2,0:T(8,128)S(1)}, f32[16,65,64]{1,2,0:T(8,128)S(1)}, u32[]{:S(2)}, u32[]{:S(2)}) %collective-permute-start.6) | collective-permute-done | bytes 266272 | tf_op jit(solution)/shard_map/ppermute | solution.py:16
  243.8 13.7 %collective-permute-start.7 = (f32[16,65,64]{1,2,0:T(8,128)S(1)}, f32[16,65,64]{1,2,0:T(8,128)S(1)}, u32[]{:S(2)}, u32[]{:S(2)}) collective-permute-start(f32[16,65,64]{1,2,0:T(8,128)S(1)} %pad_maximum_fusion.5), channel_id=1, source_target_pairs={{0,128},{4,132},{8,136},{12,140},{16,144},{20,148},{24,152},{28,15... | collective-permute-start | bytes 798728 | tf_op jit(solution)/shard_map/ppermute | solution.py:16
  257.5 16.5 %fusion.9 = f32[4,16,128,128]{3,2,1,0:T(8,128)} fusion(f32[4,128,16,64]{3,2,1,0:T(8,128)} %get-tuple-element.119, f32[4,128,16,64]{3,2,1,0:T(8,128)} %get-tuple-element.122), kind=kOutput, calls=%fused_computation.15 | convolution fusion | flops 805306368 | bytes 8388608 | tf_op jit(solution)/shard_map/cthd,cshd->chts/dot_general | solution.py:94
  274.3 10.6 %fusion.5 = f32[4,16,64,128]{3,2,1,0:T(8,128)S(1)} fusion(f32[4,128,16,64]{3,2,1,0:T(8,128)} %get-tuple-element.121, f32[4,16,64,64]{3,2,1,0:T(8,128)} %get-tuple-element.56, f32[16,64,64]{2,1,0:T(8,128)S(1)} %copy.151, f32[4,16,64]{2,1,0:T(8,128)S(1)} %get-tuple-element.57), kind=kOutput, calls=%fused_computation.11 | convolution fusion | flops 403177472 | bytes 5521408 | tf_op jit(solution)/shard_map/cthd,chde->cthe/dot_general | solution.py:148
  284.9 6.1 %fusion.56 = (f32[4,128,16]{1,2,0:T(8,128)S(1)}, f32[4,128,16,64]{1,3,2,0:T(8,128)S(1)}) fusion(f32[4,16,64,128]{3,2,1,0:T(8,128)S(1)} %fusion.5, f32[4,128,16,64]{1,3,2,0:T(8,128)S(1)} %copy-done.5, bf16[4,128,16,64]{1,3,2,0:T(8,128)(2,1)} %bitcast.14, f32[4,16,128,128]{3,2,1,0:T(8,128)S(1)} %copy-done.4, pred[4,128,128]{2,1,0:T(8,128)(4,1)S(1)} %compare_and_fusion), kind=kOutput, calls=%fused_computation.98 | convolution fusion | flops 808968192 | bytes 11632640 | tf_op jit(solution)/shard_map/chts,cshd->cthd/dot_general | solution.py:100
  292.1 18.4 %all_to_all.68 = bf16[4,128,1024]{1,2,0:T(8,128)(2,1)S(1)} all-to-all(bf16[4,128,1024]{1,2,0:T(8,128)(2,1)S(1)} %bitcast.86), channel_id=1, replica_groups=mesh['seq'=64,'head'=4] {'head'}, dimensions={0} | all-to-all | bytes 2097152 | tf_op jit(solution)/shard_map/all_to_all | solution.py:159
  310.5 1.5 convert_element_type.115
  312.0 3.1 copy.158
  315.0 3.2 fusion.24
  (105 shorter events, 21.2 us)
Async XLA Ops:
  0.0 36.4 %copy-start = (bf16[128,4096]{1,0:T(8,128)(2,1)S(1)}, bf16[128,4096]{1,0:T(8,128)(2,1)}, u32[]{:S(2)}) copy-start(bf16[128,4096]{1,0:T(8,128)(2,1)} %param.26) | copy-start | bytes 3145732
  0.0 6.9 %copy-start.12 = (bf16[128,4096]{1,0:T(8,128)(2,1)S(1)}, bf16[128,4096]{1,0:T(8,128)(2,1)}, u32[]{:S(2)}) copy-start(bf16[128,4096]{1,0:T(8,128)(2,1)} %param.18) | copy-start | bytes 3145732
  2.4 19.6 %all-to-all-start = ((bf16[128,4,1024]{0,2,1:T(8,128)(2,1)}), bf16[128,4,1024]{0,2,1:T(8,128)(2,1)S(1)}, u32[]{:S(2)}, u32[]{:S(2)}) async-start(bf16[128,4,1024]{0,2,1:T(8,128)(2,1)} %bitcast.1), calls=%async_computation | async-start | bytes 2097152 | tf_op jit(solution)/shard_map/all_to_all | solution.py:61
  6.9 29.5 %copy-start.15 = (f32[4096]{0:T(1024)S(1)}, f32[4096]{0:T(1024)}, u32[]{:S(2)}) copy-start(f32[4096]{0:T(1024)} %param.24) | copy-start | bytes 49156
  6.9 29.5 %copy-start.16 = (f32[4096]{0:T(1024)S(1)}, f32[4096]{0:T(1024)}, u32[]{:S(2)}) copy-start(f32[4096]{0:T(1024)} %param.23) | copy-start | bytes 49156
  22.0 18.7 %copy-start.6 = (bf16[128,4,1024]{0,2,1:T(8,128)(2,1)}, bf16[128,4,1024]{0,2,1:T(8,128)(2,1)S(1)}, u32[]{:S(2)}) copy-start(bf16[128,4,1024]{0,2,1:T(8,128)(2,1)S(1)} %all-to-all-done) | copy-start | bytes 3145732
  22.0 21.1 %all-to-all-start.2 = ((bf16[128,4,1024]{0,2,1:T(8,128)(2,1)}), bf16[128,4,1024]{0,2,1:T(8,128)(2,1)S(1)}, u32[]{:S(2)}, u32[]{:S(2)}) async-start(bf16[128,4,1024]{0,2,1:T(8,128)(2,1)} %bitcast.88), calls=%async_computation.2 | async-start | bytes 2097152 | tf_op jit(solution)/shard_map/all_to_all | solution.py:62
  26.4 10.0 %collective-permute-start = (bf16[1,4096]{1,0:T(2,128)(2,1)S(1)}, bf16[1,4096]{1,0:T(2,128)(2,1)S(1)}, u32[]{:S(2)}, u32[]{:S(2)}) collective-permute-start(bf16[1,4096]{1,0:T(2,128)(2,1)S(1)} %slice.59), channel_id=1, source_target_pairs={{0,1},{1,2},{2,3},{3,4},{4,5},{5,6},{6,7},{7,8},{8,9},{9,10},{10,1... | collective-permute-start | bytes 24584 | tf_op jit(solution)/shard_map/ppermute | solution.py:16
  40.7 7.9 %copy-start.13 = (bf16[128,4096]{1,0:T(8,128)(2,1)S(1)}, bf16[128,4096]{1,0:T(8,128)(2,1)}, u32[]{:S(2)}) copy-start(bf16[128,4096]{1,0:T(8,128)(2,1)} %param.19) | copy-start | bytes 3145732
  43.1 5.5 %copy-start.7 = (bf16[128,4,1024]{0,2,1:T(8,128)(2,1)}, bf16[128,4,1024]{0,2,1:T(8,128)(2,1)S(1)}, u32[]{:S(2)}) copy-start(bf16[128,4,1024]{0,2,1:T(8,128)(2,1)S(1)} %all-to-all-done.2) | copy-start | bytes 3145732
  43.1 21.1 %all-to-all-start.1 = ((bf16[128,4,1024]{0,2,1:T(8,128)(2,1)}), bf16[128,4,1024]{0,2,1:T(8,128)(2,1)}, u32[]{:S(2)}, u32[]{:S(2)}) async-start(bf16[128,4,1024]{0,2,1:T(8,128)(2,1)} %bitcast.5), calls=%async_computation.1 | async-start | bytes 2097152 | tf_op jit(solution)/shard_map/all_to_all | solution.py:64
  64.2 27.6 %all-to-all-start.3 = ((bf16[128,4,1024]{0,2,1:T(8,128)(2,1)}), bf16[128,4,1024]{0,2,1:T(8,128)(2,1)}, u32[]{:S(2)}, u32[]{:S(2)}) async-start(bf16[128,4,1024]{0,2,1:T(8,128)(2,1)} %bitcast.87), calls=%async_computation.3 | async-start | bytes 2097152 | tf_op jit(solution)/shard_map/all_to_all | solution.py:63
  77.9 2.1 copy-start.3
  111.5 16.9 %collective-permute-start.2 = (f32[16,65,64]{1,2,0:T(8,128)}, f32[16,65,64]{1,2,0:T(8,128)S(1)}, u32[]{:S(2)}, u32[]{:S(2)}) collective-permute-start(f32[16,65,64]{1,2,0:T(8,128)} %pad_maximum_fusion), channel_id=1, source_target_pairs={{0,8},{4,12},{8,16},{12,20},{16,24},{20,28},{24,32},{28,36},{32,40... | collective-permute-start | bytes 798728 | tf_op jit(solution)/shard_map/ppermute | solution.py:16
  114.4 18.1 %collective-permute-start.1 = (f32[16,65,64]{1,2,0:T(8,128)}, f32[16,65,64]{1,2,0:T(8,128)S(1)}, u32[]{:S(2)}, u32[]{:S(2)}) collective-permute-start(f32[16,65,64]{1,2,0:T(8,128)} %pad_maximum_fusion), channel_id=1, source_target_pairs={{0,4},{4,8},{8,12},{12,16},{16,20},{20,24},{24,28},{28,32},{32,36}... | collective-permute-start | bytes 798728 | tf_op jit(solution)/shard_map/ppermute | solution.py:16
  132.6 3.3 %copy-start.10 = (f32[16,65,64]{1,2,0:T(8,128)}, f32[16,65,64]{1,2,0:T(8,128)S(1)}, u32[]{:S(2)}) copy-start(f32[16,65,64]{1,2,0:T(8,128)S(1)} %collective-permute-done.1) | copy-start | bytes 798724
  138.3 14.5 %collective-permute-start.3 = (f32[16,65,64]{1,2,0:T(8,128)S(1)}, f32[16,65,64]{1,2,0:T(8,128)S(1)}, u32[]{:S(2)}, u32[]{:S(2)}) collective-permute-start(f32[16,65,64]{1,2,0:T(8,128)S(1)} %pad_maximum_fusion.1), channel_id=1, source_target_pairs={{0,8},{4,12},{8,16},{12,20},{16,24},{20,28},{24,32},{28,36},{32,40... | collective-permute-start | bytes 798728 | tf_op jit(solution)/shard_map/ppermute | solution.py:16
  152.7 0.8 copy-start.11
  157.4 27.4 %collective-permute-start.4 = (f32[16,65,64]{1,2,0:T(8,128)S(1)}, f32[16,65,64]{1,2,0:T(8,128)S(1)}, u32[]{:S(2)}, u32[]{:S(2)}) collective-permute-start(f32[16,65,64]{1,2,0:T(8,128)S(1)} %pad_maximum_fusion.2), channel_id=1, source_target_pairs={{0,16},{4,20},{8,24},{12,28},{16,32},{20,36},{24,40},{28,44},{32,4... | collective-permute-start | bytes 798728 | tf_op jit(solution)/shard_map/ppermute | solution.py:16
  184.8 0.8 copy-start.9
  190.3 29.7 %collective-permute-start.5 = (f32[16,65,64]{1,2,0:T(8,128)}, f32[16,65,64]{1,2,0:T(8,128)S(1)}, u32[]{:S(2)}, u32[]{:S(2)}) collective-permute-start(f32[16,65,64]{1,2,0:T(8,128)} %pad_maximum_fusion.3), channel_id=1, source_target_pairs={{0,32},{4,36},{8,40},{12,44},{16,48},{20,52},{24,56},{28,60},{32,6... | collective-permute-start | bytes 798728 | tf_op jit(solution)/shard_map/ppermute | solution.py:16
  219.9 3.3 %copy-start.8 = (f32[16,65,64]{1,2,0:T(8,128)}, f32[16,65,64]{1,2,0:T(8,128)S(1)}, u32[]{:S(2)}) copy-start(f32[16,65,64]{1,2,0:T(8,128)S(1)} %collective-permute-done.5) | copy-start | bytes 798724
  223.3 9.7 %copy-start.2 = (f32[128,4,1024]{0,2,1:T(8,128)S(1)}, f32[128,4,1024]{0,2,1:T(8,128)}, u32[]{:S(2)}) copy-start(f32[128,4,1024]{0,2,1:T(8,128)} %convert_element_type.114) | copy-start | bytes 6291460
  225.8 17.1 %collective-permute-start.6 = (f32[16,65,64]{1,2,0:T(8,128)S(1)}, f32[16,65,64]{1,2,0:T(8,128)S(1)}, u32[]{:S(2)}, u32[]{:S(2)}) collective-permute-start(f32[16,65,64]{1,2,0:T(8,128)S(1)} %pad_maximum_fusion.4), channel_id=1, source_target_pairs={{0,64},{4,68},{8,72},{12,76},{16,80},{20,84},{24,88},{28,92},{32,9... | collective-permute-start | bytes 798728 | tf_op jit(solution)/shard_map/ppermute | solution.py:16
  243.8 30.2 %collective-permute-start.7 = (f32[16,65,64]{1,2,0:T(8,128)S(1)}, f32[16,65,64]{1,2,0:T(8,128)S(1)}, u32[]{:S(2)}, u32[]{:S(2)}) collective-permute-start(f32[16,65,64]{1,2,0:T(8,128)S(1)} %pad_maximum_fusion.5), channel_id=1, source_target_pairs={{0,128},{4,132},{8,136},{12,140},{16,144},{20,148},{24,152},{28,15... | collective-permute-start | bytes 798728 | tf_op jit(solution)/shard_map/ppermute | solution.py:16
  274.3 10.6 %copy-start.4 = (f32[4,16,128,128]{3,2,1,0:T(8,128)S(1)}, f32[4,16,128,128]{3,2,1,0:T(8,128)}, u32[]{:S(2)}) copy-start(f32[4,16,128,128]{3,2,1,0:T(8,128)} %fusion.9) | copy-start | bytes 12582916
  274.3 10.6 %copy-start.5 = (f32[4,128,16,64]{1,3,2,0:T(8,128)S(1)}, f32[4,128,16,64]{1,3,2,0:T(8,128)}, u32[]{:S(2)}) copy-start(f32[4,128,16,64]{1,3,2,0:T(8,128)} %fusion) | copy-start | bytes 6291460
  312.0 3.1 copy-start.14
  312.0 6.2 %copy-start.1 = (bf16[128,4096]{1,0:T(8,128)(2,1)S(1)}, bf16[128,4096]{1,0:T(8,128)(2,1)}, u32[]{:S(2)}) copy-start(bf16[128,4096]{1,0:T(8,128)(2,1)} %param.26) | copy-start | bytes 3145732
where the time goes:
time: 320 us; the launch traced here: 318 us
  waiting for transfers between devices  90.9 us (28%)
  starting transfers between devices  64.3 us (20%)
  other arithmetic  51.7 us (16%)
  local copies, waits for them, and re-layouts  45.7 us (14%)
  matrix products  45.2 us (14%)
  blocking collectives  18.4 us (6%)
    ppermute x8, waiting for transfers between devices, shifted(): return lax.ppermute(value, axis, pairs)  76.6 us
    ppermute x8, starting transfers between devices, shifted(): return lax.ppermute(value, axis, pairs)  46.5 us
    all_to_all x1, blocking collectives, local(): lax.all_to_all(normed, 'head', split_axis=0, concat_axis=1, tiled=True)  18.4 us
    dot_general x1, matrix products, local(): jnp.einsum('cthd,cshd->chts', scaled_query, scaled_key, precision=highest)  16.5 us
    all_to_all x1, waiting for transfers between devices, local(): lax.all_to_all(acceptance_linear, 'head', split_axis=1, concat_axis=0, ti...  13.8 us
    unnamed x42, local copies, waits for them, and re-layouts  11.8 us
    mul x1, other arithmetic, local(): scaled_key = lookup_vectors * jnp.exp(-cumulative)  11.3 us
    dot_general x1, matrix products, local(): jnp.einsum('cthd,chde->cthe', scaled_query * keep_first[:, :, None, None]...  10.6 us
  transfers between devices with their start and end apart: 12, of which 9 were waited for; matrix products, arithmetic and copies ran while one was open for 22% of the time, Pallas kernels for 0%

commit v1 on v0

--- a/solution.py
+++ b/solution.py
@@ -57,8 +57,17 @@
         decay_hidden_rows, fading_raise_map, preferred_element_type=jnp.float32
     )
     log_decay = jnp.maximum(-jnp.exp(decay_score), decay_floor).astype(jnp.bfloat16)
+    enter_the_target = lambda original, mesh_name: jnp.concatenate(
+        jax.lax.all_to_all(
+            jnp.stack(jnp.split(original, jax.lax.axis_size(mesh_name), 1)),
+            axis_name=mesh_name,
+            split_axis=0,
+            concat_axis=0,
+        ),
+        0,
+    )
     query_head, key_head, value_head, decay_head = (
-        lax.all_to_all(acceptance_linear, "head", split_axis=1, concat_axis=0, tiled=True),
+        enter_the_target(acceptance_linear, "head"),
         lax.all_to_all(lookup_linear, "head", split_axis=1, concat_axis=0, tiled=True),
         lax.all_to_all(payload_linear, "head", split_axis=1, concat_axis=0, tiled=True),
         lax.all_to_all(log_decay, "head", split_axis=1, concat_axis=0, tiled=True),

time: 320 us -> 320 us (level)
  the two profiles are of different devices: /device:TPU:162 before, /device:TPU:2 now
where the time goes in v1:
time: 320 us; the launch traced here: 318 us
  waiting for transfers between devices  108 us (34%)
  local copies, waits for them, and re-layouts  52.9 us (17%)
  other arithmetic  48.1 us (15%)
  matrix products  44.2 us (14%)
  starting transfers between devices  43.8 us (14%)
  blocking collectives  18.7 us (6%)
    ppermute x8, waiting for transfers between devices, shifted(): return lax.ppermute(value, axis, pairs)  95.1 us
    ppermute x8, starting transfers between devices, shifted(): return lax.ppermute(value, axis, pairs)  26 us
    all_to_all x1, blocking collectives, local(): lax.all_to_all(normed, 'head', split_axis=0, concat_axis=1, tiled=True)  18.7 us
    unnamed x57, local copies, waits for them, and re-layouts  17.9 us
    dot_general x1, matrix products, local(): jnp.einsum('cthd,cshd->chts', scaled_query, scaled_key, precision=highest)  16.4 us
    dot_general x1, matrix products, local(): jnp.einsum('cthd,chde->cthe', scaled_query * keep_first[:, :, None, None]...  10.3 us
    all_to_all x1, waiting for transfers between devices, local(): lax.all_to_all(lookup_linear, 'head', split_axis=1, concat_axis=0, tiled=...  9.45 us
    mul x1, other arithmetic, local(): scaled_key = lookup_vectors * jnp.exp(-cumulative)  8.27 us
  transfers between devices with their start and end apart: 12, of which 9 were waited for; matrix products, arithmetic and copies ran while one was open for 21% of the time, Pallas kernels for 0%

profile of v1, /device:TPU:2, one launch (start us, length us, event | category | flops | bytes accessed | tf_op | source)
XLA Modules:
  0.0 317.8 jit_solution(11915021360664976711)
XLA Ops:
  0.0 2.4 copy.142
  2.4 4.5 %all-to-all-start.2 = ((bf16[128,4,1024]{0,2,1:T(8,128)(2,1)}), bf16[128,4,1024]{0,2,1:T(8,128)(2,1)S(1)}, u32[]{:S(2)}, u32[]{:S(2)}) async-start(bf16[128,4,1024]{0,2,1:T(8,128)(2,1)} %bitcast.11), calls=%async_computation.2 | async-start | bytes 2097152 | tf_op jit(solution)/shard_map/all_to_all | solution.py:71
  7.8 1.1 copy.173
  8.9 1.1 copy.172
  10.1 1.1 copy.171
  11.4 1.1 pad_maximum_fusion
  12.5 9.5 %all-to-all-done.2 = bf16[128,4,1024]{0,2,1:T(8,128)(2,1)S(1)} async-done(((bf16[128,4,1024]{0,2,1:T(8,128)(2,1)}), bf16[128,4,1024]{0,2,1:T(8,128)(2,1)S(1)}, u32[]{:S(2)}, u32[]{:S(2)}) %all-to-all-start.2) | async-done | bytes 1048608 | tf_op jit(solution)/shard_map/all_to_all | solution.py:71
  22.9 3.5 %all-to-all-start = ((bf16[4,128,1024]{1,2,0:T(8,128)(2,1)}), bf16[4,128,1024]{1,2,0:T(8,128)(2,1)S(1)}, u32[]{:S(2)}, u32[]{:S(2)}) async-start(bf16[4,128,1024]{1,2,0:T(8,128)(2,1)} %pad_maximum_fusion), calls=%async_computation | async-start | bytes 2097152 | tf_op jit(solution)/shard_map/all_to_all | solution.py:61
  26.5 3.9 %collective-permute-start = (bf16[1,4096]{1,0:T(2,128)(2,1)S(1)}, bf16[1,4096]{1,0:T(2,128)(2,1)S(1)}, u32[]{:S(2)}, u32[]{:S(2)}) collective-permute-start(bf16[1,4096]{1,0:T(2,128)(2,1)S(1)} %slice.59), channel_id=1, source_target_pairs={{0,1},{1,2},{2,3},{3,4},{4,5},{5,6},{6,7},{7,8},{8,9},{9,10},{10,1... | collective-permute-start | bytes 24584 | tf_op jit(solution)/shard_map/ppermute | solution.py:16
  31.2 1.4 fusion.57
  34.0 3.4 %collective-permute-done = bf16[1,4096]{1,0:T(2,128)(2,1)S(1)} collective-permute-done((bf16[1,4096]{1,0:T(2,128)(2,1)S(1)}, bf16[1,4096]{1,0:T(2,128)(2,1)S(1)}, u32[]{:S(2)}, u32[]{:S(2)}) %collective-permute-start) | collective-permute-done | bytes 8224 | tf_op jit(solution)/shard_map/ppermute | solution.py:16
  37.4 3.6 %fusion.4 = bf16[128,4096]{1,0:T(8,128)(2,1)} fusion(bf16[128,4096]{1,0:T(8,128)(2,1)S(1)} %copy-done, bf16[4096,128]{1,0:T(8,128)(2,1)} %param.25, bf16[128,4096]{1,0:T(8,128)(2,1)S(1)} %copy-done.20, bf16[127,4096]{1,0:T(8,128)(2,1)S(1)} %bitcast.97, bf16[1,4096]{1,0:T(2,128)(2,1)S(1)} %collective-permute-done, f32[4096]{0:T(1024)S(1)} %copy-done.21, ...), kind=kOutput, calls=%fused_computation.10 | convolution fusion | flops 276316160 | bytes 5275776 | tf_op jit(solution)/shard_map/dot_general | solution.py:56
  41.0 2.3 copy.167
  43.3 5.5 %all-to-all-start.1 = ((bf16[128,4,1024]{0,2,1:T(8,128)(2,1)}), bf16[128,4,1024]{0,2,1:T(8,128)(2,1)}, u32[]{:S(2)}, u32[]{:S(2)}) async-start(bf16[128,4,1024]{0,2,1:T(8,128)(2,1)} %bitcast.7), calls=%async_computation.1 | async-start | bytes 2097152 | tf_op jit(solution)/shard_map/all_to_all | solution.py:73
  48.8 1.3 copy.168
  52.7 1.4 convert_element_type.109
  54.0 3.0 copy.143
  57.0 3.6 %copy.141 = f32[4,128,16,64]{3,2,1,0:T(8,128)} copy(bf16[4,128,16,64]{1,3,2,0:T(8,128)(2,1)} %bitcast.84) | data formatting | bytes 3145728 | tf_op jit(solution)/shard_map/convert_element_type | solution.py:94
  60.6 3.8 %all-to-all-done.1 = bf16[128,4,1024]{0,2,1:T(8,128)(2,1)} async-done(((bf16[128,4,1024]{0,2,1:T(8,128)(2,1)}), bf16[128,4,1024]{0,2,1:T(8,128)(2,1)}, u32[]{:S(2)}, u32[]{:S(2)}) %all-to-all-start.1) | async-done | bytes 1048608 | tf_op jit(solution)/shard_map/all_to_all | solution.py:73
  64.5 4.3 %all-to-all-start.3 = ((bf16[128,4,1024]{0,2,1:T(8,128)(2,1)}), bf16[128,4,1024]{0,2,1:T(8,128)(2,1)}, u32[]{:S(2)}, u32[]{:S(2)}) async-start(bf16[128,4,1024]{0,2,1:T(8,128)(2,1)} %bitcast.89), calls=%async_computation.3 | async-start | bytes 2097152 | tf_op jit(solution)/shard_map/all_to_all | solution.py:72
  68.7 2.7 convert_element_type.108
  71.5 4.1 %copy.139 = f32[4,128,16,64]{3,2,1,0:T(8,128)} copy(f32[4,128,16,64]{1,3,2,0:T(8,128)} %bitcast.86) | data formatting | bytes 4194304 | tf_op jit(solution)/shard_map/convert_element_type | solution.py:97
  75.5 2.7 fusion.59
  79.0 1.3 copy-done.3
  80.3 8.3 %exponential_multiply_fusion = (f32[4,128,16,64]{3,2,1,0:T(8,128)}, f32[4,128,16,64]{3,2,1,0:T(8,128)}, f32[4,128,16,64]{3,2,1,0:T(8,128)}, f32[4,128,16,64]{3,2,1,0:T(8,128)}) fusion(f32[4,128,16,64]{3,2,1,0:T(8,128)} %copy.143, f32[4,128,16,64]{3,2,1,0:T(8,128)S(1)} %fusion.59, f32[4,128]{1,0:T(4,128)S(1)} %get-tuple-element.129, ...), kind=kLoop, calls=%fused_computation.21 | loop fusion | flops 4194304 | bytes 16797696 | tf_op jit(solution)/shard_map/mul | solution.py:102
  88.5 7.8 %fusion.7 = f32[4,16,64,64]{3,2,1,0:T(8,128)} fusion(bf16[4,128,16,64]{1,3,2,0:T(8,128)(2,1)} %bitcast.16, f32[4,128,16,64]{3,2,1,0:T(8,128)} %get-tuple-element.120), kind=kOutput, calls=%fused_computation.13 | convolution fusion | flops 402653184 | bytes 4194304 | tf_op jit(solution)/shard_map/cthd,cthe->chde/dot_general | solution.py:116
  96.3 8.9 %while.26 = (s32[]{:T(128)}, f32[16,64,64]{2,1,0:T(8,128)S(1)}, f32[4,16,64,64]{3,2,1,0:T(8,128)}, f32[4,16,64]{2,1,0:T(8,128)S(1)}, f32[4,16,64,64]{3,2,1,0:T(8,128)}, /*index=5*/s32[]{:T(128)}, s32[]{:T(128)}) while((s32[]{:T(128)}, f32[16,64,64]{2,1,0:T(8,128)S(1)}, f32[4,16,64,64]{3,2,1,0:T(8,128)}, ...), condition=%wide.region_3.4_spmd.clone, body=%wide.region_2.3_spmd.clone.sunk | while | flops 262147 | bytes 1585260 | solution.py:126
  97.2 1.3 bitcast_add_fusion.4
  99.4 1.3 bitcast_add_fusion.4
  101.6 1.3 bitcast_add_fusion.4
  103.8 1.3 bitcast_add_fusion.4
  106.6 2.1 pad_maximum_fusion.1
  108.7 1.9 collective-permute-start.1
  110.6 4.0 %collective-permute-start.2 = (f32[16,65,64]{1,2,0:T(8,128)}, f32[16,65,64]{1,2,0:T(8,128)S(1)}, u32[]{:S(2)}, u32[]{:S(2)}) collective-permute-start(f32[16,65,64]{1,2,0:T(8,128)} %pad_maximum_fusion.1), channel_id=1, source_target_pairs={{0,8},{4,12},{8,16},{12,20},{16,24},{20,28},{24,32},{28,36},{32,40... | collective-permute-start | bytes 798728 | tf_op jit(solution)/shard_map/ppermute | solution.py:16
  114.6 9.6 %collective-permute-done.1 = f32[16,65,64]{1,2,0:T(8,128)S(1)} collective-permute-done((f32[16,65,64]{1,2,0:T(8,128)}, f32[16,65,64]{1,2,0:T(8,128)S(1)}, u32[]{:S(2)}, u32[]{:S(2)}) %collective-permute-start.1) | collective-permute-done | bytes 266272 | tf_op jit(solution)/shard_map/ppermute | solution.py:16
  125.2 1.2 copy.174
  126.4 5.1 %collective-permute-done.2 = f32[16,65,64]{1,2,0:T(8,128)S(1)} collective-permute-done((f32[16,65,64]{1,2,0:T(8,128)}, f32[16,65,64]{1,2,0:T(8,128)S(1)}, u32[]{:S(2)}, u32[]{:S(2)}) %collective-permute-start.2) | collective-permute-done | bytes 266272 | tf_op jit(solution)/shard_map/ppermute | solution.py:16
  132.5 1.2 copy.175
  136.0 1.2 pad_maximum_fusion.2
  137.2 1.9 collective-permute-start.3
  139.2 16.0 %collective-permute-done.3 = f32[16,65,64]{1,2,0:T(8,128)S(1)} collective-permute-done((f32[16,65,64]{1,2,0:T(8,128)S(1)}, f32[16,65,64]{1,2,0:T(8,128)S(1)}, u32[]{:S(2)}, u32[]{:S(2)}) %collective-permute-start.3) | collective-permute-done | bytes 266272 | tf_op jit(solution)/shard_map/ppermute | solution.py:16
  156.2 1.2 copy.176
  158.6 1.1 fusion.48
  159.7 1.2 pad_maximum_fusion.3
  161.0 1.9 collective-permute-start.4
  162.9 26.6 %collective-permute-done.4 = f32[16,65,64]{1,2,0:T(8,128)S(1)} collective-permute-done((f32[16,65,64]{1,2,0:T(8,128)S(1)}, f32[16,65,64]{1,2,0:T(8,128)S(1)}, u32[]{:S(2)}, u32[]{:S(2)}) %collective-permute-start.4) | collective-permute-done | bytes 266272 | tf_op jit(solution)/shard_map/ppermute | solution.py:16
  190.5 1.2 copy.177
  194.0 2.2 pad_maximum_fusion.4
  196.2 4.6 %collective-permute-start.5 = (f32[16,65,64]{1,2,0:T(8,128)}, f32[16,65,64]{1,2,0:T(8,128)S(1)}, u32[]{:S(2)}, u32[]{:S(2)}) collective-permute-start(f32[16,65,64]{1,2,0:T(8,128)} %pad_maximum_fusion.4), channel_id=1, source_target_pairs={{0,32},{4,36},{8,40},{12,44},{16,48},{20,52},{24,56},{28,60},{32,6... | collective-permute-start | bytes 798728 | tf_op jit(solution)/shard_map/ppermute | solution.py:16
  203.2 23.9 %collective-permute-done.5 = f32[16,65,64]{1,2,0:T(8,128)S(1)} collective-permute-done((f32[16,65,64]{1,2,0:T(8,128)}, f32[16,65,64]{1,2,0:T(8,128)S(1)}, u32[]{:S(2)}, u32[]{:S(2)}) %collective-permute-start.5) | collective-permute-done | bytes 266272 | tf_op jit(solution)/shard_map/ppermute | solution.py:16
  229.0 1.3 copy.178
  231.4 1.3 fusion.46
  233.4 1.2 pad_maximum_fusion.5
  234.7 3.5 %collective-permute-start.6 = (f32[16,65,64]{1,2,0:T(8,128)S(1)}, f32[16,65,64]{1,2,0:T(8,128)S(1)}, u32[]{:S(2)}, u32[]{:S(2)}) collective-permute-start(f32[16,65,64]{1,2,0:T(8,128)S(1)} %pad_maximum_fusion.5), channel_id=1, source_target_pairs={{0,64},{4,68},{8,72},{12,76},{16,80},{20,84},{24,88},{28,92},{32,9... | collective-permute-start | bytes 798728 | tf_op jit(solution)/shard_map/ppermute | solution.py:16
  238.2 1.7 fusion
  240.0 10.5 %collective-permute-done.6 = f32[16,65,64]{1,2,0:T(8,128)S(1)} collective-permute-done((f32[16,65,64]{1,2,0:T(8,128)S(1)}, f32[16,65,64]{1,2,0:T(8,128)S(1)}, u32[]{:S(2)}, u32[]{:S(2)}) %collective-permute-start.6) | collective-permute-done | bytes 266272 | tf_op jit(solution)/shard_map/ppermute | solution.py:16
  253.3 4.3 %collective-permute-start.7 = (f32[16,65,64]{1,2,0:T(8,128)S(1)}, f32[16,65,64]{1,2,0:T(8,128)S(1)}, u32[]{:S(2)}, u32[]{:S(2)}) collective-permute-start(f32[16,65,64]{1,2,0:T(8,128)S(1)} %pad_maximum_fusion.6), channel_id=1, source_target_pairs={{0,128},{4,132},{8,136},{12,140},{16,144},{20,148},{24,152},{28,15... | collective-permute-start | bytes 798728 | tf_op jit(solution)/shard_map/ppermute | solution.py:16
  257.6 16.4 %fusion.9 = f32[4,16,128,128]{3,2,1,0:T(8,128)} fusion(f32[4,128,16,64]{3,2,1,0:T(8,128)} %get-tuple-element.119, f32[4,128,16,64]{3,2,1,0:T(8,128)} %get-tuple-element.122), kind=kOutput, calls=%fused_computation.15 | convolution fusion | flops 805306368 | bytes 8388608 | tf_op jit(solution)/shard_map/cthd,cshd->chts/dot_general | solution.py:103
  274.9 1.2 copy.162
  276.1 10.3 %fusion.5 = f32[4,16,64,128]{3,2,1,0:T(8,128)S(1)} fusion(f32[4,128,16,64]{3,2,1,0:T(8,128)} %get-tuple-element.121, f32[4,16,64,64]{3,2,1,0:T(8,128)S(1)} %copy-done.12, f32[16,64,64]{2,1,0:T(8,128)S(1)} %copy.162, f32[4,16,64]{2,1,0:T(8,128)S(1)} %get-tuple-element.57), kind=kOutput, calls=%fused_computation.11 | convolution fusion | flops 403177472 | bytes 5521408 | tf_op jit(solution)/shard_map/cthd,chde->cthe/dot_general | solution.py:157
  286.4 6.1 %fusion.58 = (f32[4,128,16]{1,2,0:T(8,128)S(1)}, f32[4,128,16,64]{1,3,2,0:T(8,128)S(1)}) fusion(f32[4,16,64,128]{3,2,1,0:T(8,128)S(1)} %fusion.5, f32[4,128,16,64]{1,3,2,0:T(8,128)S(1)} %copy-done.7, bf16[4,128,16,64]{1,3,2,0:T(8,128)(2,1)} %bitcast.16, f32[4,16,128,128]{3,2,1,0:T(8,128)S(1)} %copy-done.4, pred[4,128,128]{2,1,0:T(8,128)(4,1)S(1)} %compare_and_fusion), kind=kOutput, calls=%fused_computation.101 | convolution fusion | flops 808968192 | bytes 11632640 | tf_op jit(solution)/shard_map/chts,cshd->cthd/dot_general | solution.py:109
  293.7 18.7 %all_to_all.60 = bf16[4,128,1024]{1,2,0:T(8,128)(2,1)S(1)} all-to-all(bf16[4,128,1024]{1,2,0:T(8,128)(2,1)S(1)} %bitcast.88), channel_id=1, replica_groups=mesh['seq'=64,'head'=4] {'head'}, dimensions={0} | all-to-all | bytes 2097152 | tf_op jit(solution)/shard_map/all_to_all | solution.py:168
  312.5 1.9 copy.169
  314.4 3.4 %fusion.24 = bf16[128,4096]{1,0:T(8,128)(2,1)} fusion(f32[128,4096]{1,0:T(8,128)} %copy.169, bf16[128,4096]{1,0:T(8,128)(2,1)} %param.20), kind=kLoop, calls=%fused_computation.43 | loop fusion | flops 3670016 | bytes 4194304 | tf_op jit(solution)/shard_map/convert_element_type | solution.py:169
  (121 shorter events, 32.0 us)
Async XLA Ops:
  0.0 37.4 %copy-start = (bf16[128,4096]{1,0:T(8,128)(2,1)S(1)}, bf16[128,4096]{1,0:T(8,128)(2,1)}, u32[]{:S(2)}) copy-start(bf16[128,4096]{1,0:T(8,128)(2,1)} %param.26) | copy-start | bytes 3145732
  0.0 6.9 %copy-start.18 = (bf16[128,4096]{1,0:T(8,128)(2,1)S(1)}, bf16[128,4096]{1,0:T(8,128)(2,1)}, u32[]{:S(2)}) copy-start(bf16[128,4096]{1,0:T(8,128)(2,1)} %param.17) | copy-start | bytes 3145732
  2.4 19.6 %all-to-all-start.2 = ((bf16[128,4,1024]{0,2,1:T(8,128)(2,1)}), bf16[128,4,1024]{0,2,1:T(8,128)(2,1)S(1)}, u32[]{:S(2)}, u32[]{:S(2)}) async-start(bf16[128,4,1024]{0,2,1:T(8,128)(2,1)} %bitcast.11), calls=%async_computation.2 | async-start | bytes 2097152 | tf_op jit(solution)/shard_map/all_to_all | solution.py:71
  11.4 26.0 %copy-start.21 = (f32[4096]{0:T(1024)S(1)}, f32[4096]{0:T(1024)}, u32[]{:S(2)}) copy-start(f32[4096]{0:T(1024)} %param.24) | copy-start | bytes 49156
  11.4 26.0 %copy-start.22 = (f32[4096]{0:T(1024)S(1)}, f32[4096]{0:T(1024)}, u32[]{:S(2)}) copy-start(f32[4096]{0:T(1024)} %param.23) | copy-start | bytes 49156
  12.5 14.0 %copy-start.20 = (bf16[128,4096]{1,0:T(8,128)(2,1)S(1)}, bf16[128,4096]{1,0:T(8,128)(2,1)}, u32[]{:S(2)}) copy-start(bf16[128,4096]{1,0:T(8,128)(2,1)} %param.21) | copy-start | bytes 3145732
  22.0 1.0 copy-start.11
  22.9 20.4 %all-to-all-start = ((bf16[4,128,1024]{1,2,0:T(8,128)(2,1)}), bf16[4,128,1024]{1,2,0:T(8,128)(2,1)S(1)}, u32[]{:S(2)}, u32[]{:S(2)}) async-start(bf16[4,128,1024]{1,2,0:T(8,128)(2,1)} %pad_maximum_fusion), calls=%async_computation | async-start | bytes 2097152 | tf_op jit(solution)/shard_map/all_to_all | solution.py:61
  26.5 10.9 %collective-permute-start = (bf16[1,4096]{1,0:T(2,128)(2,1)S(1)}, bf16[1,4096]{1,0:T(2,128)(2,1)S(1)}, u32[]{:S(2)}, u32[]{:S(2)}) collective-permute-start(bf16[1,4096]{1,0:T(2,128)(2,1)S(1)} %slice.59), channel_id=1, source_target_pairs={{0,1},{1,2},{2,3},{3,4},{4,5},{5,6},{6,7},{7,8},{8,9},{9,10},{10,1... | collective-permute-start | bytes 24584 | tf_op jit(solution)/shard_map/ppermute | solution.py:16
  41.0 7.8 %copy-start.19 = (bf16[128,4096]{1,0:T(8,128)(2,1)S(1)}, bf16[128,4096]{1,0:T(8,128)(2,1)}, u32[]{:S(2)}) copy-start(bf16[128,4096]{1,0:T(8,128)(2,1)} %param.19) | copy-start | bytes 3145732
  43.3 6.8 %copy-start.5 = (bf16[4,128,1024]{1,2,0:T(8,128)(2,1)}, bf16[4,128,1024]{1,2,0:T(8,128)(2,1)S(1)}, u32[]{:S(2)}) copy-start(bf16[4,128,1024]{1,2,0:T(8,128)(2,1)S(1)} %all-to-all-done) | copy-start | bytes 3145732
  43.3 21.1 %all-to-all-start.1 = ((bf16[128,4,1024]{0,2,1:T(8,128)(2,1)}), bf16[128,4,1024]{0,2,1:T(8,128)(2,1)}, u32[]{:S(2)}, u32[]{:S(2)}) async-start(bf16[128,4,1024]{0,2,1:T(8,128)(2,1)} %bitcast.7), calls=%async_computation.1 | async-start | bytes 2097152 | tf_op jit(solution)/shard_map/all_to_all | solution.py:73
  64.5 24.1 %all-to-all-start.3 = ((bf16[128,4,1024]{0,2,1:T(8,128)(2,1)}), bf16[128,4,1024]{0,2,1:T(8,128)(2,1)}, u32[]{:S(2)}, u32[]{:S(2)}) async-start(bf16[128,4,1024]{0,2,1:T(8,128)(2,1)} %bitcast.89), calls=%async_computation.3 | async-start | bytes 2097152 | tf_op jit(solution)/shard_map/all_to_all | solution.py:72
  75.5 3.4 %copy-start.2 = (f32[4,128,16,64]{3,2,1,0:T(8,128)S(1)}, f32[4,128,16,64]{3,2,1,0:T(8,128)}, u32[]{:S(2)}) copy-start(f32[4,128,16,64]{3,2,1,0:T(8,128)} %copy.139) | copy-start | bytes 6291460
  75.5 4.7 %copy-start.3 = (f32[4,128,16,64]{3,2,1,0:T(8,128)S(1)}, f32[4,128,16,64]{3,2,1,0:T(8,128)}, u32[]{:S(2)}) copy-start(f32[4,128,16,64]{3,2,1,0:T(8,128)} %copy.141) | copy-start | bytes 6291460
  108.7 15.5 %collective-permute-start.1 = (f32[16,65,64]{1,2,0:T(8,128)}, f32[16,65,64]{1,2,0:T(8,128)S(1)}, u32[]{:S(2)}, u32[]{:S(2)}) collective-permute-start(f32[16,65,64]{1,2,0:T(8,128)} %pad_maximum_fusion.1), channel_id=1, source_target_pairs={{0,4},{4,8},{8,12},{12,16},{16,20},{20,24},{24,28},{28,32},{32,36}... | collective-permute-start | bytes 798728 | tf_op jit(solution)/shard_map/ppermute | solution.py:16
  110.6 20.9 %collective-permute-start.2 = (f32[16,65,64]{1,2,0:T(8,128)}, f32[16,65,64]{1,2,0:T(8,128)S(1)}, u32[]{:S(2)}, u32[]{:S(2)}) collective-permute-start(f32[16,65,64]{1,2,0:T(8,128)} %pad_maximum_fusion.1), channel_id=1, source_target_pairs={{0,8},{4,12},{8,16},{12,20},{16,24},{20,28},{24,32},{28,36},{32,40... | collective-permute-start | bytes 798728 | tf_op jit(solution)/shard_map/ppermute | solution.py:16
  131.5 3.4 %copy-start.16 = (f32[16,65,64]{1,2,0:T(8,128)}, f32[16,65,64]{1,2,0:T(8,128)S(1)}, u32[]{:S(2)}) copy-start(f32[16,65,64]{1,2,0:T(8,128)S(1)} %collective-permute-done.2) | copy-start | bytes 798724
  137.2 18.0 %collective-permute-start.3 = (f32[16,65,64]{1,2,0:T(8,128)S(1)}, f32[16,65,64]{1,2,0:T(8,128)S(1)}, u32[]{:S(2)}, u32[]{:S(2)}) collective-permute-start(f32[16,65,64]{1,2,0:T(8,128)S(1)} %pad_maximum_fusion.2), channel_id=1, source_target_pairs={{0,8},{4,12},{8,16},{12,20},{16,24},{20,28},{24,32},{28,36},{32,40... | collective-permute-start | bytes 798728 | tf_op jit(solution)/shard_map/ppermute | solution.py:16
  155.2 2.3 copy-start.17
  161.0 28.5 %collective-permute-start.4 = (f32[16,65,64]{1,2,0:T(8,128)S(1)}, f32[16,65,64]{1,2,0:T(8,128)S(1)}, u32[]{:S(2)}, u32[]{:S(2)}) collective-permute-start(f32[16,65,64]{1,2,0:T(8,128)S(1)} %pad_maximum_fusion.3), channel_id=1, source_target_pairs={{0,16},{4,20},{8,24},{12,28},{16,32},{20,36},{24,40},{28,44},{32,4... | collective-permute-start | bytes 798728 | tf_op jit(solution)/shard_map/ppermute | solution.py:16
  189.5 3.4 %copy-start.15 = (f32[16,65,64]{1,2,0:T(8,128)}, f32[16,65,64]{1,2,0:T(8,128)S(1)}, u32[]{:S(2)}) copy-start(f32[16,65,64]{1,2,0:T(8,128)S(1)} %collective-permute-done.4) | copy-start | bytes 798724
  194.0 33.2 %copy-start.8 = (f32[16,64,64]{1,2,0:T(8,128)}, f32[16,64,64]{1,2,0:T(8,128)S(1)}, u32[]{:S(2)}) copy-start(f32[16,64,64]{1,2,0:T(8,128)S(1)} %fusion.47) | copy-start | bytes 786436
  196.2 31.0 %collective-permute-start.5 = (f32[16,65,64]{1,2,0:T(8,128)}, f32[16,65,64]{1,2,0:T(8,128)S(1)}, u32[]{:S(2)}, u32[]{:S(2)}) collective-permute-start(f32[16,65,64]{1,2,0:T(8,128)} %pad_maximum_fusion.4), channel_id=1, source_target_pairs={{0,32},{4,36},{8,40},{12,44},{16,48},{20,52},{24,56},{28,60},{32,6... | collective-permute-start | bytes 798728 | tf_op jit(solution)/shard_map/ppermute | solution.py:16
  227.2 0.8 copy-start.13
  229.0 9.2 %copy-start.6 = (bf16[4,128,1024]{1,2,0:T(8,128)(2,1)S(1)}, bf16[4,128,1024]{1,2,0:T(8,128)(2,1)}, u32[]{:S(2)}) copy-start(bf16[4,128,1024]{1,2,0:T(8,128)(2,1)} %copy-done.5) | copy-start | bytes 3145732
  232.6 0.8 copy-start.9
  234.7 15.8 %collective-permute-start.6 = (f32[16,65,64]{1,2,0:T(8,128)S(1)}, f32[16,65,64]{1,2,0:T(8,128)S(1)}, u32[]{:S(2)}, u32[]{:S(2)}) collective-permute-start(f32[16,65,64]{1,2,0:T(8,128)S(1)} %pad_maximum_fusion.5), channel_id=1, source_target_pairs={{0,64},{4,68},{8,72},{12,76},{16,80},{20,84},{24,88},{28,92},{32,9... | collective-permute-start | bytes 798728 | tf_op jit(solution)/shard_map/ppermute | solution.py:16
  240.0 12.0 %copy-start.10 = (f32[16,64,64]{1,2,0:T(8,128)S(1)}, f32[16,64,64]{1,2,0:T(8,128)}, u32[]{:S(2)}) copy-start(f32[16,64,64]{1,2,0:T(8,128)} %copy-done.9) | copy-start | bytes 786436
  250.4 0.8 copy-start.14
  253.3 20.7 %collective-permute-start.7 = (f32[16,65,64]{1,2,0:T(8,128)S(1)}, f32[16,65,64]{1,2,0:T(8,128)S(1)}, u32[]{:S(2)}, u32[]{:S(2)}) collective-permute-start(f32[16,65,64]{1,2,0:T(8,128)S(1)} %pad_maximum_fusion.6), channel_id=1, source_target_pairs={{0,128},{4,132},{8,136},{12,140},{16,144},{20,148},{24,152},{28,15... | collective-permute-start | bytes 798728 | tf_op jit(solution)/shard_map/ppermute | solution.py:16
  274.0 2.1 copy-start.12
  276.1 10.3 %copy-start.4 = (f32[4,16,128,128]{3,2,1,0:T(8,128)S(1)}, f32[4,16,128,128]{3,2,1,0:T(8,128)}, u32[]{:S(2)}) copy-start(f32[4,16,128,128]{3,2,1,0:T(8,128)} %fusion.9) | copy-start | bytes 12582916
  276.1 10.3 %copy-start.7 = (f32[4,128,16,64]{1,3,2,0:T(8,128)S(1)}, f32[4,128,16,64]{1,3,2,0:T(8,128)}, u32[]{:S(2)}) copy-start(f32[4,128,16,64]{1,3,2,0:T(8,128)} %fusion) | copy-start | bytes 6291460
  312.5 5.3 %copy-start.1 = (bf16[128,4096]{1,0:T(8,128)(2,1)S(1)}, bf16[128,4096]{1,0:T(8,128)(2,1)}, u32[]{:S(2)}) copy-start(bf16[128,4096]{1,0:T(8,128)(2,1)} %param.26) | copy-start | bytes 3145732
